TPU v7x, 32 devices: a whole 2x2x4 slice. The times are simulated.
32 devices in a mesh: groups: 2 (over y), tensor: 4 (over z), seq: 2 (over x), load: 2 (over core).
Axes of the slice: x: 2, y: 2, z: 4, core: 2. Of those that a mesh axis runs over, the one named last changes fastest.
Arguments:
- tokens: bfloat16 [1024, 16384], P(('groups', 'tensor'), ('seq', 'load')), parts along dimension 0, may hold values from -21 to 21
- weight_query: bfloat16 [16384, 16384], P(('seq', 'load'), 'tensor'), may hold values from -0.046875 to 0.046875
- weight_keyval: bfloat16 [16384, 2048], P(('seq', 'load'), 'tensor'), may hold values from -0.046875 to 0.046875
- down_query: bfloat16 [16384, 1024], P(('seq', 'load'), ('groups', 'tensor')), parts along dimension 1, may hold values from -0.046875 to 0.046875
- down_keyval: bfloat16 [16384, 1024], P(('seq', 'load'), ('groups', 'tensor')), parts along dimension 1, may hold values from -0.046875 to 0.046875
- up_query: bfloat16 [1024, 16384], P(('groups', 'load'), 'tensor'), parts along dimension 0, may hold values from -0.5 to 0.5
- up_keyval: bfloat16 [1024, 2048], P(('groups', 'load'), 'tensor'), parts along dimension 0, may hold values from -0.5 to 0.5
- adapter_rank: int32 [8], P('groups'), parts along dimension 0, may hold values from 8 to 128, as said below
- token_lengths: int32 [8], P('groups'), parts along dimension 0, may hold values from 1 to 384, 512 in all
- adapter_slot: int32 [8], P('groups'), parts along dimension 0, may hold values from 0 to 3, each once
Outputs:
- context: bfloat16 [1024, 16384], P(('groups', 'seq', 'load'), 'tensor'), parts along dimension 0
- kv_cache: bfloat16 [1024, 2048], P(('groups', 'seq', 'load'), 'tensor'), parts along dimension 0
There are 2 independent parts, one for each index of `groups`. A program takes and returns all parts, laid end to end along the dimension named above; an argument that names none is the same for every part. Nothing has to cross between parts.
Inputs may be any that keep to these rules, and one draw needn't show every extreme that they name: `adapter_rank`: each rank is a power of two; some tenant has rank 128 and some has rank 8. `token_lengths`: the lengths sum to 512; some tenant has exactly 384 tokens. `adapter_slot`: each slot belongs to exactly one tenant.
All inputs are finite; a program needn't handle non-finite values.
Results may differ from a plain program's by a relative error of at most 0.0025.
The roundings to bfloat16 on the way count: a program that leaves them out, or rounds other values in their place, can miss the bound.
Values may be sent and summed in bfloat16 or wider, within the bound.
No kernel may reach another device: no remote copies, remote signals or barrier semaphores. Data moves between devices by JAX's collectives and lax.ppermute only.
A program may use at most 128 MiB of HBM per device.

v0:
```python
import math
import jax
import jax.numpy as jnp
from jax import lax
from jax.sharding import PartitionSpec as P

HEADS = 128
KV_HEADS = 8
HEAD_DIM = 128
TENANTS = 4
ROPE_BASE = 500000.0
ADAPTER_ALPHA = 8.0


def product(left, right):
    return jnp.dot(left, right, preferred_element_type=jnp.float32)


def rotate_pairs(values, position, first_col):
    cols = values.shape[1]
    width = HEAD_DIM if cols % HEAD_DIM == 0 else cols
    col = jnp.arange(width, dtype=jnp.int32)
    pair_col = first_col + col - col % 2
    within = pair_col % HEAD_DIM // 2
    frequency = jnp.exp(-(2.0 * within.astype(jnp.float32) / HEAD_DIM) * math.log(ROPE_BASE))
    angles = position.astype(jnp.float32)[:, None] * frequency[None, :]
    cosine = jnp.cos(angles)
    sine_angle = jnp.sin(angles)
    signed_sine = jnp.where((col % 2 == 0)[None, :], -sine_angle, sine_angle)
    cosine, signed_sine = lax.optimization_barrier((cosine, signed_sine))
    cosine = jnp.tile(cosine, (1, cols // width))
    signed_sine = jnp.tile(signed_sine, (1, cols // width))
    is_even = (jnp.arange(cols, dtype=jnp.int32) % 2 == 0)[None, :]
    partner = jnp.where(is_even, jnp.roll(values, -1, axis=1), jnp.roll(values, 1, axis=1))
    return values * cosine + partner * signed_sine


def tenant_table(token_ids, adapter_rank, token_lengths, adapter_slot):
    segment_ends = jnp.cumsum(token_lengths)
    begins = segment_ends - token_lengths
    owned_rows = (token_ids[:, None] >= begins[None, :]) & (
        token_ids[:, None] < segment_ends[None, :]
    )
    zero_int = jnp.zeros((), jnp.int32)
    own_rank = jnp.sum(jnp.where(owned_rows, adapter_rank[None, :], zero_int), axis=1)
    own_slot = jnp.sum(jnp.where(owned_rows, adapter_slot[None, :], zero_int), axis=1)
    own_first = jnp.sum(jnp.where(owned_rows, begins[None, :], zero_int), axis=1)
    slot_hot = own_slot[:, None] == jnp.arange(TENANTS, dtype=jnp.int32)[None, :]
    return (own_rank, own_first, slot_hot)


def select_slot(down_values, slot_hot):
    shaped = down_values.reshape(down_values.shape[0], -1, TENANTS)
    return jnp.sum(jnp.where(slot_hot[:, None, :], shaped, 0.0), axis=2)


def scale_ranks(picked, own_rank, first_rank):
    rank_index = first_rank + jnp.arange(picked.shape[1], dtype=jnp.int32)
    keep_mask = rank_index[None, :] < own_rank[:, None]
    factor = ADAPTER_ALPHA / jnp.sqrt(own_rank.astype(jnp.float32))
    return jnp.where(keep_mask, picked * factor[:, None], 0.0).astype(jnp.bfloat16)


def widen_slots(low_values, slot_hot):
    wide_rows = jnp.where(
        slot_hot[:, None, :], low_values[:, :, None], jnp.zeros((), low_values.dtype)
    )
    return wide_rows.reshape(low_values.shape[0], -1)


def ring_reduce_scatter(blocks, axis):
    count = lax.axis_size(axis)
    me = lax.axis_index(axis)
    if count == 1:
        return blocks[0]
    shift = [(i, (i + 1) % count) for i in range(count)]

    def pick(step):
        return lax.dynamic_index_in_dim(blocks, (me - 1 - step) % count, 0, keepdims=False)

    total = pick(0)
    for step in range(1, count):
        total = lax.ppermute(total, axis, shift) + pick(step)
    return total


def shards(
    tokens,
    weight_query,
    weight_keyval,
    down_query,
    down_keyval,
    up_query,
    up_keyval,
    adapter_rank,
    token_lengths,
    adapter_slot,
):
    tensor_count = lax.axis_size("tensor")
    block_count = lax.axis_size(("seq", "load"))
    tensor_index = lax.axis_index("tensor")
    block_index = lax.axis_index(("seq", "load"))
    query_cols = weight_query.shape[1]
    keyval_cols = weight_keyval.shape[1]
    rank_share = down_query.shape[1] // TENANTS
    block_rows = tokens.shape[0] * tensor_count // block_count
    up_query_all = lax.all_gather(up_query, "load", axis=0, tiled=True)
    up_keyval_all = lax.all_gather(up_keyval, "load", axis=0, tiled=True)
    ring = tensor_count
    chunk = tokens.shape[0]
    small_cols = keyval_cols + 2 * rank_share
    small_terms = jnp.zeros((ring, chunk, small_cols), jnp.float32)
    query_terms = jnp.zeros((ring, chunk, query_cols), jnp.float32)
    shift = [(i, (i + 1) % ring) for i in range(ring)]
    held = tokens
    for step in range(ring):
        following = lax.ppermute(held, "tensor", shift) if step < ring - 1 else None
        owner = (tensor_index - step) % ring
        block_ids = owner * chunk + jnp.arange(chunk, dtype=jnp.int32)
        _, _, block_hot = tenant_table(block_ids, adapter_rank, token_lengths, adapter_slot)
        small_block = jnp.concatenate(
            [
                product(held, weight_keyval),
                select_slot(product(held, down_query), block_hot),
                select_slot(product(held, down_keyval), block_hot),
            ],
            axis=1,
        )
        small_terms = lax.dynamic_update_slice_in_dim(small_terms, small_block[None], owner, 0)
        if step == 0 and ring > 2:
            first_block, first_owner = (held, owner)
        elif step == 1 and ring > 2:
            pair = product(jnp.concatenate([first_block, held], axis=0), weight_query)
            query_terms = lax.dynamic_update_slice_in_dim(
                query_terms, pair[:chunk][None], first_owner, 0
            )
            query_terms = lax.dynamic_update_slice_in_dim(query_terms, pair[chunk:][None], owner, 0)
        else:
            query_terms = lax.dynamic_update_slice_in_dim(
                query_terms, product(held, weight_query)[None], owner, 0
            )
        if following is not None:
            if step == 0 and ring > 2:
                following, small_terms, first_block = lax.optimization_barrier(
                    (following, small_terms, first_block)
                )
            else:
                following, small_terms, query_terms = lax.optimization_barrier(
                    (following, small_terms, query_terms)
                )
        held = following
    seq_count = lax.axis_size("seq")
    load_count = lax.axis_size("load")
    by_core = small_terms.reshape(seq_count, load_count, block_rows, -1)
    per_core = ring_reduce_scatter(jnp.moveaxis(by_core, 1, 0), "load")
    small_summed = ring_reduce_scatter(per_core, "seq")
    query_summed = lax.psum_scatter(
        query_terms.reshape(ring * chunk, -1), ("seq", "load"), scatter_dimension=0, tiled=True
    )
    token_ids = block_index * block_rows + jnp.arange(block_rows, dtype=jnp.int32)
    own_rank, own_first, slot_hot = tenant_table(
        token_ids, adapter_rank, token_lengths, adapter_slot
    )
    position = token_ids - own_first
    first_rank = tensor_index * rank_share
    low_query = scale_ranks(
        small_summed[:, keyval_cols : keyval_cols + rank_share], own_rank, first_rank
    )
    low_keyval = scale_ranks(small_summed[:, keyval_cols + rank_share :], own_rank, first_rank)
    low_both = lax.all_gather(jnp.concatenate([low_query, low_keyval], axis=1), "tensor", axis=1)
    full_query = low_both[:, :, :rank_share].reshape(block_rows, -1)
    full_keyval = low_both[:, :, rank_share:].reshape(block_rows, -1)
    wide_query = widen_slots(full_query, slot_hot)
    wide_keyval = widen_slots(full_keyval, slot_hot)
    delta_keyval = product(wide_keyval, up_keyval_all)
    keyval = small_summed[:, :keyval_cols] + delta_keyval
    kv_first_col = tensor_index * keyval_cols
    is_key = kv_first_col + jnp.arange(keyval_cols, dtype=jnp.int32) < KV_HEADS * HEAD_DIM
    kv_local = jnp.where(
        is_key[None, :], rotate_pairs(keyval, position, kv_first_col), keyval
    ).astype(jnp.bfloat16)
    kv_all = lax.all_gather(kv_local, "tensor", axis=1, tiled=True)
    heads_here = query_cols // HEAD_DIM
    group_size = HEADS // KV_HEADS
    kv_here = max(heads_here // group_size, 1)
    per_kv = heads_here // kv_here
    kv_first = tensor_index * heads_here // group_size
    key_cols = KV_HEADS * HEAD_DIM
    key_heads = lax.dynamic_slice_in_dim(
        kv_all, kv_first * HEAD_DIM, kv_here * HEAD_DIM, 1
    ).reshape(block_rows, kv_here, HEAD_DIM)
    value_heads = lax.dynamic_slice_in_dim(
        kv_all, key_cols + kv_first * HEAD_DIM, kv_here * HEAD_DIM, 1
    ).reshape(block_rows, kv_here, HEAD_DIM)
    both_heads = lax.all_gather(
        jnp.concatenate([key_heads, value_heads], axis=1), ("seq", "load"), axis=0, tiled=True
    )
    piece_keys = both_heads[:, :kv_here]
    piece_values = both_heads[:, kv_here:]
    delta_query = lax.optimization_barrier(product(wide_query, up_query_all))
    query_rows = rotate_pairs(
        query_summed + delta_query, position, tensor_index * query_cols
    ).astype(jnp.bfloat16)
    grouped = query_rows.reshape(block_rows, kv_here, per_kv, HEAD_DIM)
    key_ids = jnp.arange(piece_keys.shape[0], dtype=jnp.int32)
    visible = (key_ids[None, :] >= own_first[:, None]) & (key_ids[None, :] <= token_ids[:, None])
    scores = jnp.einsum(
        "qghd,kgd->ghqk", grouped, piece_keys, preferred_element_type=jnp.float32
    ) / math.sqrt(HEAD_DIM)
    scores = jnp.where(visible, scores, -1e30)
    row_top = jnp.max(scores, axis=3)
    exp_scores = jnp.where(visible, jnp.exp(scores - row_top[..., None]), 0.0)
    row_total = jnp.sum(exp_scores, axis=3)
    accumulated = jnp.einsum(
        "ghqk,kgd->ghqd",
        exp_scores.astype(jnp.bfloat16),
        piece_values,
        preferred_element_type=jnp.float32,
    )
    context = (accumulated / row_total[..., None]).astype(jnp.bfloat16)
    context = jnp.transpose(context, (2, 0, 1, 3)).reshape(block_rows, query_cols)
    return (context, kv_local)


def solution(mesh):
    placed = (
        P(("groups", "tensor"), ("seq", "load")),
        P(("seq", "load"), "tensor"),
        P(("seq", "load"), "tensor"),
        P(("seq", "load"), ("groups", "tensor")),
        P(("seq", "load"), ("groups", "tensor")),
        P(("groups", "load"), "tensor"),
        P(("groups", "load"), "tensor"),
        P("groups"),
        P("groups"),
        P("groups"),
    )
    return jax.shard_map(
        shards,
        mesh=mesh,
        in_specs=placed,
        out_specs=(P(("groups", "seq", "load"), "tensor"), P(("groups", "seq", "load"), "tensor")),
        check_vma=False,
    )
```

profile of v0, /device:TPU:0, one launch (start us, length us, event | category | flops | bytes accessed | tf_op | source)
XLA Modules:
  0.0 206.6 jit_solution(1513930682166711280)
XLA Ops:
  8.1 3.1 %collective-permute-start = (bf16[128,4096]{1,0:T(8,128)(2,1)}, bf16[128,4096]{1,0:T(8,128)(2,1)}, u32[]{:S(2)}, u32[]{:S(2)}) collective-permute-start(bf16[128,4096]{1,0:T(8,128)(2,1)} %param.10), channel_id=1, source_target_pairs={{0,4},{4,8},{8,12},{12,0},{1,5},{5,9},{9,13},{13,1},{2,6},{6,10},{... | collective-permute-start | bytes 3145736 | tf_op jit(solution)/shard_map/ppermute | solution.py:117
  12.9 1.7 fusion.49
  16.1 2.9 %fusion.48 = f32[128,512]{1,0:T(8,128)S(1)} fusion(bf16[128,4096]{1,0:T(8,128)(2,1)S(1)} %copy-done.5, bf16[4096,512]{1,0:T(8,128)(2,1)} %param.12), kind=kOutput, calls=%fused_computation.146 | convolution fusion | flops 536870912 | bytes 5505024 | tf_op jit(solution)/shard_map/dot_general | solution.py:16
  21.2 15.5 %collective-permute-done = bf16[128,4096]{1,0:T(8,128)(2,1)} collective-permute-done((bf16[128,4096]{1,0:T(8,128)(2,1)}, bf16[128,4096]{1,0:T(8,128)(2,1)}, u32[]{:S(2)}, u32[]{:S(2)}) %collective-permute-start) | collective-permute-done | bytes 1048608 | tf_op jit(solution)/shard_map/ppermute | solution.py:117
  36.7 1.7 fusion.52
  38.4 1.7 fusion.53
  40.2 2.8 %fusion.51 = f32[128,512]{1,0:T(8,128)} fusion(bf16[128,4096]{1,0:T(8,128)(2,1)} %collective-permute-done, bf16[4096,512]{1,0:T(8,128)(2,1)S(1)} %copy-done.1), kind=kOutput, calls=%fused_computation.149 | convolution fusion | flops 536870912 | bytes 5505024 | tf_op jit(solution)/shard_map/dot_general | solution.py:16
  45.9 15.3 %fusion.13 = f32[256,4096]{1,0:T(8,128)S(1)} fusion(bf16[4096,4096]{1,0:T(8,128)(2,1)} %param.11, bf16[128,4096]{1,0:T(8,128)(2,1)} %collective-permute-done, bf16[128,4096]{1,0:T(8,128)(2,1)S(1)} %copy-done.6), kind=kOutput, calls=%fused_computation.21 | convolution fusion | flops 8594128896 | bytes 39845888 | tf_op jit(solution)/shard_map/dot_general | solution.py:16
  61.2 4.3 %broadcast_in_dim.276 = f32[4,128,4096]{2,1,0:T(8,128)} broadcast(f32[]{:T(128)} %constant.193.clone.1), dimensions={} | broadcast | bytes 8388612 | tf_op jit(solution)/shard_map/broadcast_in_dim | solution.py:113
  70.5 14.2 %fusion.3 = f32[4,128,4096]{2,1,0:T(8,128)} fusion(f32[4,128,4096]{2,1,0:T(8,128)} %fusion.11, s32[]{:T(128)S(6)} %select_n.264, bf16[128,4096]{1,0:T(8,128)(2,1)S(1)} %collective-permute-done.1, bf16[4096,4096]{1,0:T(8,128)(2,1)} %param.11), kind=kOutput, calls=%fused_computation.7 | convolution fusion | flops 4294967296 | bytes 36700164 | tf_op jit(solution)/shard_map/dot_general | solution.py:16
  86.8 2.9 %fusion.54 = f32[128,512]{1,0:T(8,128)S(1)} fusion(bf16[128,4096]{1,0:T(8,128)(2,1)S(1)} %collective-permute-done.1, bf16[4096,512]{1,0:T(8,128)(2,1)} %param.12), kind=kOutput, calls=%fused_computation.152 | convolution fusion | flops 536870912 | bytes 5505024 | tf_op jit(solution)/shard_map/dot_general | solution.py:16
  92.4 3.0 %collective-permute-done.2 = bf16[128,4096]{1,0:T(8,128)(2,1)S(1)} collective-permute-done((bf16[128,4096]{1,0:T(8,128)(2,1)S(1)}, bf16[128,4096]{1,0:T(8,128)(2,1)S(1)}, u32[]{:S(2)}, u32[]{:S(2)}) %collective-permute-start.2) | collective-permute-done | bytes 1048608 | tf_op jit(solution)/shard_map/ppermute | solution.py:117
  95.4 14.2 %fusion.2 = f32[4,128,4096]{2,1,0:T(8,128)} fusion(f32[4,128,4096]{2,1,0:T(8,128)} %fusion.3, s32[]{:T(128)S(6)} %select_n.269, bf16[128,4096]{1,0:T(8,128)(2,1)S(1)} %collective-permute-done.2, bf16[4096,4096]{1,0:T(8,128)(2,1)} %param.11), kind=kOutput, calls=%fused_computation.5 | convolution fusion | flops 4294967296 | bytes 36700164 | tf_op jit(solution)/shard_map/dot_general | solution.py:16
  111.7 2.9 %fusion.57 = f32[128,512]{1,0:T(8,128)S(1)} fusion(bf16[128,4096]{1,0:T(8,128)(2,1)S(1)} %collective-permute-done.2, bf16[4096,512]{1,0:T(8,128)(2,1)} %param.12), kind=kOutput, calls=%fused_computation.155 | convolution fusion | flops 536870912 | bytes 5505024 | tf_op jit(solution)/shard_map/dot_general | solution.py:16
  118.1 2.6 %all_gather.20 = bf16[512,512]{1,0:T(8,128)(2,1)S(1)} all-gather(bf16[256,512]{1,0:T(8,128)(2,1)S(1)} %copy-done.10), channel_id=1, replica_groups=mesh['groups'=2,'tensor'=4,'seq'=2,'load'=2] {'load'}, dimensions={0}, use_global_device_ids=true | all-gather | bytes 786432 | tf_op jit(solution)/shard_map/all_gather | solution.py:108
  124.3 7.8 %collective-permute-done.4 = f32[128,576]{1,0:T(8,128)S(1)} collective-permute-done((f32[128,576]{1,0:T(8,128)S(1)}, f32[128,576]{1,0:T(8,128)S(1)}, u32[]{:S(2)}, u32[]{:S(2)}) %collective-permute-start.4) | collective-permute-done | bytes 294944 | tf_op jit(solution)/shard_map/ppermute | solution.py:83
  132.4 13.1 %all-gather = bf16[128,256]{0,1:T(8,128)(2,1)S(1)} all-gather(bf16[128,64]{0,1:T(8,128)(2,1)S(1)} %copy.81), channel_id=2, replica_groups=mesh['groups'=2,'tensor'=4,'seq'=2,'load'=2] {'tensor'}, dimensions={1}, use_global_device_ids=true | all-gather | bytes 81920 | tf_op jit(solution)/shard_map/all_gather | solution.py:170
  146.5 15.0 %all_gather.21 = bf16[128,2048]{1,0:T(8,128)(2,1)S(1)} all-gather(bf16[128,512]{1,0:T(8,128)(2,1)S(1)} %fusion.25), channel_id=1, replica_groups=mesh['groups'=2,'tensor'=4,'seq'=2,'load'=2] {'tensor'}, dimensions={1}, use_global_device_ids=true | all-gather | bytes 655360 | tf_op jit(solution)/shard_map/all_gather | solution.py:182
  162.1 11.1 %all_gather.22 = bf16[512,4,128]{2,0,1:T(8,128)(2,1)} all-gather(bf16[128,4,128]{2,0,1:T(8,128)(2,1)S(1)} %pad_maximum_fusion), channel_id=1, replica_groups=mesh['groups'=2,'tensor'=4,'seq'=2,'load'=2] {'seq','load'}, dimensions={0}, use_global_device_ids=true | all-gather | bytes 655360 | tf_op jit(solution)/shard_map/all_gather | solution.py:195
  173.2 2.9 %fusion.60 = f32[128,4096]{1,0:T(8,128)S(1)} fusion(bf16[128,512]{0,1:T(8,128)(2,1)S(1)} %bitcast.152, bf16[512,4096]{1,0:T(8,128)(2,1)} %all-gather.3.cloned.1.call-done), kind=kOutput, calls=%fused_computation.158 | convolution fusion | flops 536870912 | bytes 6422528 | tf_op jit(solution)/shard_map/dot_general | solution.py:16
  176.1 7.4 %reduce-scatter.2.cloned.1.call-done = f32[128,4096]{1,0:T(8,128)} async-done(((f32[512,4096]{1,0:T(8,128)}), f32[128,4096]{1,0:T(8,128)}) %reduce-scatter.2.cloned.1.call-update) | async-done | bytes 2097168 | tf_op jit(solution)/shard_map/reduce_scatter | solution.py:157
  183.6 1.8 add.313
  186.5 4.4 %fusion.22 = bf16[16,8,32,128]{3,1,2,0:T(8,128)(2,1)S(1)} fusion(f32[16,8,32,128]{3,2,1,0:T(8,128)S(1)} %bitcast.148, f32[128,4095]{1,0:T(8,128)S(1)} %get-tuple-element.58, f32[128,1]{1,0:T(8,128)S(1)} %get-tuple-element.60, f32[128,1]{1,0:T(8,128)S(1)} %get-tuple-element.59, f32[128,4095]{1,0:T(8,128)S(1)} %get-tuple-element.57, f32[128,4096]{1,0:T(8,128)S(1)} %add.313, ...), kind=kLoop, calls=%fused_computation.30 | loop fusion | flops 3670016 | bytes 11538432
  192.4 4.6 %fusion.47 = (f32[2,16,128]{2,1,0:T(8,128)S(1)}, bf16[2,16,128,512]{2,3,1,0:T(8,128)(2,1)S(1)}) fusion(f32[2,512,128,16]{2,1,3,0:T(8,128)S(1)} %fusion.20, pred[128,512]{0,1:T(8,128)(4,1)S(1)} %copy-done.12), kind=kOutput, calls=%fused_computation.145 | output fusion | flops 16777728 | bytes 12664832 | tf_op jit(solution)/shard_map/sub | solution.py:212
  (132 shorter events, 33.1 us)
Async XLA Ops:
  8.0 4.9 %copy-start = (bf16[4096,128]{1,0:T(8,128)(2,1)S(1)}, bf16[4096,128]{1,0:T(8,128)(2,1)}, u32[]{:S(2)}) copy-start(bf16[4096,128]{1,0:T(8,128)(2,1)} %param.13) | copy-start | bytes 3145732
  8.0 6.6 %copy-start.5 = (bf16[128,4096]{1,0:T(8,128)(2,1)S(1)}, bf16[128,4096]{1,0:T(8,128)(2,1)}, u32[]{:S(2)}) copy-start(bf16[128,4096]{1,0:T(8,128)(2,1)} %param.10) | copy-start | bytes 3145732
  8.0 6.6 %copy-start.2 = (bf16[4096,128]{1,0:T(8,128)(2,1)S(1)}, bf16[4096,128]{1,0:T(8,128)(2,1)}, u32[]{:S(2)}) copy-start(bf16[4096,128]{1,0:T(8,128)(2,1)} %param.14) | copy-start | bytes 3145732
  8.0 7.2 %copy-start.17 = (s32[4]{0:T(128)S(1)}, s32[4]{0:T(128)}, u32[]{:S(2)}) copy-start(s32[4]{0:T(128)} %param.17) | copy-start | bytes 52
  8.0 7.2 %copy-start.18 = (s32[4]{0:T(128)S(1)}, s32[4]{0:T(128)}, u32[]{:S(2)}) copy-start(s32[4]{0:T(128)} %param.19) | copy-start | bytes 52
  8.1 165.1 %all-gather.3.cloned.1.call-start = ((), (), s32[]{:S(2)}) async-start(), calls=%async_computation.2 | async-start | bytes 6291456 | tf_op jit(solution)/shard_map/all_gather | solution.py:107
  8.1 28.6 %collective-permute-start = (bf16[128,4096]{1,0:T(8,128)(2,1)}, bf16[128,4096]{1,0:T(8,128)(2,1)}, u32[]{:S(2)}, u32[]{:S(2)}) collective-permute-start(bf16[128,4096]{1,0:T(8,128)(2,1)} %param.10), channel_id=1, source_target_pairs={{0,4},{4,8},{8,12},{12,0},{1,5},{5,9},{9,13},{13,1},{2,6},{6,10},{... | collective-permute-start | bytes 3145736 | tf_op jit(solution)/shard_map/ppermute | solution.py:117
  11.2 172.4 %reduce-scatter.2.cloned.1.call-start = ((), (), s32[]{:S(2)}) async-start(), calls=%async_computation.1 | async-start | bytes 10485760 | tf_op jit(solution)/shard_map/reduce_scatter | solution.py:157
  19.3 20.9 %copy-start.1 = (bf16[4096,512]{1,0:T(8,128)(2,1)S(1)}, bf16[4096,512]{1,0:T(8,128)(2,1)}, u32[]{:S(2)}) copy-start(bf16[4096,512]{1,0:T(8,128)(2,1)} %param.12) | copy-start | bytes 12582916
  40.2 5.7 %copy-start.6 = (bf16[128,4096]{1,0:T(8,128)(2,1)S(1)}, bf16[128,4096]{1,0:T(8,128)(2,1)}, u32[]{:S(2)}) copy-start(bf16[128,4096]{1,0:T(8,128)(2,1)} %param.10) | copy-start | bytes 3145732
  43.0 26.4 %collective-permute-start.1 = (bf16[128,4096]{1,0:T(8,128)(2,1)}, bf16[128,4096]{1,0:T(8,128)(2,1)S(1)}, u32[]{:S(2)}, u32[]{:S(2)}) collective-permute-start(bf16[128,4096]{1,0:T(8,128)(2,1)} %collective-permute-done), channel_id=1, source_target_pairs={{0,4},{4,8},{8,12},{12,0},{1,5},{5,9},{9,13},{13,1},{2,6},{6,10},{... | collective-permute-start | bytes 3145736 | tf_op jit(solution)/shard_map/ppermute | solution.py:117
  65.5 1.5 copy-start.8
  69.3 16.0 %copy-start.3 = (bf16[4096,128]{1,0:T(8,128)(2,1)S(1)}, bf16[4096,128]{1,0:T(8,128)(2,1)}, u32[]{:S(2)}) copy-start(bf16[4096,128]{1,0:T(8,128)(2,1)} %param.14) | copy-start | bytes 3145732
  69.4 26.1 %collective-permute-start.2 = (bf16[128,4096]{1,0:T(8,128)(2,1)S(1)}, bf16[128,4096]{1,0:T(8,128)(2,1)S(1)}, u32[]{:S(2)}, u32[]{:S(2)}) collective-permute-start(bf16[128,4096]{1,0:T(8,128)(2,1)S(1)} %collective-permute-done.1), channel_id=1, source_target_pairs={{0,4},{4,8},{8,12},{12,0},{1,5},{5,9},{9,13},{13,1},{2,6},{6,10},{... | collective-permute-start | bytes 3145736 | tf_op jit(solution)/shard_map/ppermute | solution.py:117
  86.8 2.9 %copy-start.11 = (f32[128,32]{1,0:T(8,128)S(1)}, f32[128,32]{1,0:T(8,128)}, u32[]{:S(2)}) copy-start(f32[128,32]{1,0:T(8,128)} %copy.74) | copy-start | bytes 49156
  109.7 1.2 copy-start.4
  111.7 6.4 %copy-start.10 = (bf16[256,512]{1,0:T(8,128)(2,1)S(1)}, bf16[256,512]{1,0:T(8,128)(2,1)}, u32[]{:S(2)}) copy-start(bf16[256,512]{1,0:T(8,128)(2,1)} %param.16) | copy-start | bytes 786436
  116.8 3.8 %collective-permute-start.3 = (f32[2,128,576]{1,2,0:T(8,128)S(1)}, f32[2,128,576]{1,2,0:T(8,128)S(1)}, u32[]{:S(2)}, u32[]{:S(2)}) collective-permute-start(f32[2,128,576]{1,2,0:T(8,128)S(1)} %dynamic-slice_bitcast_fusion), channel_id=1, source_target_pairs={{0,1},{1,0},{2,3},{3,2},{4,5},{5,4},{6,7},{7,6},{8,9},{9,8},{10,11... | collective-permute-start | bytes 1769480 | tf_op jit(solution)/shard_map/ppermute | solution.py:83
  122.0 24.3 %copy-start.15 = (pred[512]{0:T(512)(128)(4,1)S(1)}, pred[512]{0:T(512)(128)(4,1)}, u32[]{:S(2)}) copy-start(pred[512]{0:T(512)(128)(4,1)} %get-tuple-element.87) | copy-start | bytes 1540
  122.0 24.3 %copy-start.16 = (pred[512]{0:T(512)(128)(4,1)S(1)}, pred[512]{0:T(512)(128)(4,1)}, u32[]{:S(2)}) copy-start(pred[512]{0:T(512)(128)(4,1)} %get-tuple-element.88) | copy-start | bytes 1540
  122.2 9.8 %collective-permute-start.4 = (f32[128,576]{1,0:T(8,128)S(1)}, f32[128,576]{1,0:T(8,128)S(1)}, u32[]{:S(2)}, u32[]{:S(2)}) collective-permute-start(f32[128,576]{1,0:T(8,128)S(1)} %bitcast.154), channel_id=1, source_target_pairs={{0,2},{2,0},{1,3},{3,1},{4,6},{6,4},{5,7},{7,5},{8,10},{10,8},{9,1... | collective-permute-start | bytes 884744 | tf_op jit(solution)/shard_map/ppermute | solution.py:83
  146.5 29.6 %copy-start.9 = (bf16[128,512]{1,0:T(8,128)(2,1)}, bf16[128,512]{1,0:T(8,128)(2,1)S(1)}, u32[]{:S(2)}) copy-start(bf16[128,512]{1,0:T(8,128)(2,1)S(1)} %fusion.25) | copy-start | bytes 393220
  186.5 4.6 %copy-start.7 = (bf16[512,4,128]{2,0,1:T(8,128)(2,1)S(1)}, bf16[512,4,128]{2,0,1:T(8,128)(2,1)}, u32[]{:S(2)}) copy-start(bf16[512,4,128]{2,0,1:T(8,128)(2,1)} %all_gather.22) | copy-start | bytes 1572868
  191.1 1.3 copy-start.12
  (2 other events, 1.2 us)
Sparse Core Ops, SparseCore 0:
  11.3 15.5 all-gather.2
Sparse Core Ops, SparseCore 1:
  109.8 73.7 reduce-scatter.1
where the time goes:
time: 207 us
  matrix products  68.5 us (33%)
  blocking collectives  41.8 us (20%)
  waiting for transfers between devices  33.8 us (16%)
  local copies, waits for them, and re-layouts  22.2 us (11%)
  other arithmetic  18.4 us (9%)
  between operations  16.3 us (8%)
  starting transfers between devices  5.62 us (3%)
    dot_general x17, matrix products, product(): return jnp.dot(left, right, preferred_element_type=jnp.float32)  66.4 us
    ppermute x3, waiting for transfers between devices, shards(): following = lax.ppermute(held, 'tensor', shift) if step < ring - 1 else None  18.6 us
    all_gather x1, blocking collectives, shards(): kv_all = lax.all_gather(kv_local, 'tensor', axis=1, tiled=True)  15 us
    all_gather x1, blocking collectives, shards(): lax.all_gather(jnp.concatenate([low_query, low_keyval], axis=1), 'tensor'...  13.1 us
    all_gather x1, blocking collectives, shards(): lax.all_gather(jnp.concatenate([key_heads, value_heads], axis=1), ('seq',...  11.1 us
    ppermute x2, waiting for transfers between devices, ring_reduce_scatter(): total = lax.ppermute(total, axis, shift) + pick(step)  7.78 us
    reduce_scatter x1, waiting for transfers between devices, shards(): lax.psum_scatter(query_terms.reshape(ring * chunk, -1), ('seq', 'load'),...  7.43 us
    sub x1, other arithmetic, shards(): exp_scores = jnp.where(visible, jnp.exp(scores - row_top[..., None]), 0.0)  4.59 us
  transfers between devices with their start and end apart: 7, of which 5 were waited for; matrix products, arithmetic and copies ran while one was open for 45% of the time, Pallas kernels for 0%

commit v1 on v0

--- a/solution.py
+++ b/solution.py
@@ -1,8 +1,10 @@
+import functools
 import math
 import jax
 import jax.numpy as jnp
 from jax import lax
 from jax.sharding import PartitionSpec as P
+from jax.lax import axis_index, axis_size, ppermute
 
 HEADS = 128
 KV_HEADS = 8
@@ -10,6 +12,24 @@
 TENANTS = 4
 ROPE_BASE = 500000.0
 ADAPTER_ALPHA = 8.0
+
+
+def play_clusters_for(a0, join_dim):
+    num_devices = axis_size(("seq", "load"))
+    by_place = [(p, (p + 1) % num_devices) for p in range(num_devices)]
+    frames = [(p, (p - 1) % num_devices) for p in range(num_devices)]
+    y, newest = ([a0], [a0])
+    for _ in range(num_devices // 2):
+        y.append(ppermute(y[-1], ("seq", "load"), by_place))
+    for _ in [*range((num_devices - 1) // 2)]:
+        newest.append(ppermute(newest[-1], ("seq", "load"), frames))
+    y1 = jnp.concatenate([*y[::-1], *newest[1:]], join_dim)
+    return jnp.roll(
+        y1, (axis_index(("seq", "load")) - num_devices // 2) * a0.shape[join_dim], join_dim
+    )
+
+
+open_racks_for = functools.partial(play_clusters_for, join_dim=0)
 
 
 def product(left, right):
@@ -192,9 +212,7 @@
     value_heads = lax.dynamic_slice_in_dim(
         kv_all, key_cols + kv_first * HEAD_DIM, kv_here * HEAD_DIM, 1
     ).reshape(block_rows, kv_here, HEAD_DIM)
-    both_heads = lax.all_gather(
-        jnp.concatenate([key_heads, value_heads], axis=1), ("seq", "load"), axis=0, tiled=True
-    )
+    both_heads = open_racks_for(jnp.concatenate([key_heads, value_heads], axis=1))
     piece_keys = both_heads[:, :kv_here]
     piece_values = both_heads[:, kv_here:]
     delta_query = lax.optimization_barrier(product(wide_query, up_query_all))

time: 207 us -> 213 us (1.029)
  blocking collectives: 41.8 us -> 31.2 us
  local copies, waits for them, and re-layouts: 22.2 us -> 29.9 us
  waiting for transfers between devices: 33.8 us -> 37 us
    all_gather x1 -> x0, blocking collectives: 11.1 us -> none  [shards(): lax.all_gather(jnp.concatenate([key_heads, value_heads], axis=1), ('seq',...]
    ppermute x0 -> x3, waiting for transfers between devices: none -> 10 us  [the longest x2 10 us: play_clusters_for(): y.append(ppermute(y[-1], ('seq', 'load'), by_place))]
    reduce_scatter x1, waiting for transfers between devices: 7.43 us -> 0.01 us  [shards(): lax.psum_scatter(query_terms.reshape(ring * chunk, -1), ('seq', 'load'),...]
    unnamed x40 -> x43, local copies, waits for them, and re-layouts: 2.23 us -> 8.37 us
    unnamed x1 -> x3, other arithmetic: 4.37 us -> 5.72 us
  transfers between devices with their start and end apart: 7 -> 10, of which waited for: 5 -> 6; matrix products, arithmetic and copies ran while one was open for 45% -> 48% of each run, Pallas kernels for 0% -> 0%
where the time goes in v1:
time: 213 us
  matrix products  70.4 us (33%)
  waiting for transfers between devices  37 us (17%)
  blocking collectives  31.2 us (15%)
  local copies, waits for them, and re-layouts  29.9 us (14%)
  other arithmetic  20.4 us (10%)
  between operations  16.2 us (8%)
  starting transfers between devices  7.38 us (3%)
    dot_general x17, matrix products, product(): return jnp.dot(left, right, preferred_element_type=jnp.float32)  66.4 us
    ppermute x3, waiting for transfers between devices, shards(): following = lax.ppermute(held, 'tensor', shift) if step < ring - 1 else None  18.6 us
    all_gather x1, blocking collectives, shards(): kv_all = lax.all_gather(kv_local, 'tensor', axis=1, tiled=True)  15.5 us
    all_gather x1, blocking collectives, shards(): lax.all_gather(jnp.concatenate([low_query, low_keyval], axis=1), 'tensor'...  13.1 us
    ppermute x2, waiting for transfers between devices, play_clusters_for(): y.append(ppermute(y[-1], ('seq', 'load'), by_place))  10 us
    ppermute x2, waiting for transfers between devices, ring_reduce_scatter(): total = lax.ppermute(total, axis, shift) + pick(step)  8.41 us
    unnamed x43, local copies, waits for them, and re-layouts  8.37 us
    unnamed x3, other arithmetic  5.72 us
  transfers between devices with their start and end apart: 10, of which 6 were waited for; matrix products, arithmetic and copies ran while one was open for 48% of the time, Pallas kernels for 0%

profile of v1, /device:TPU:0, one launch (start us, length us, event | category | flops | bytes accessed | tf_op | source)
XLA Modules:
  0.0 212.6 jit_solution(14028036621463900106)
XLA Ops:
  8.1 3.1 %collective-permute-start = (bf16[128,4096]{1,0:T(8,128)(2,1)}, bf16[128,4096]{1,0:T(8,128)(2,1)}, u32[]{:S(2)}, u32[]{:S(2)}) collective-permute-start(bf16[128,4096]{1,0:T(8,128)(2,1)} %param.10), channel_id=1, source_target_pairs={{0,4},{4,8},{8,12},{12,0},{1,5},{5,9},{9,13},{13,1},{2,6},{6,10},{... | collective-permute-start | bytes 3145736 | tf_op jit(solution)/shard_map/ppermute | solution.py:137
  12.9 1.7 fusion.51
  16.1 2.9 %fusion.50 = f32[128,512]{1,0:T(8,128)S(1)} fusion(bf16[128,4096]{1,0:T(8,128)(2,1)S(1)} %copy-done.5, bf16[4096,512]{1,0:T(8,128)(2,1)} %param.12), kind=kOutput, calls=%fused_computation.156 | convolution fusion | flops 536870912 | bytes 5505024 | tf_op jit(solution)/shard_map/dot_general | solution.py:36
  21.2 15.5 %collective-permute-done = bf16[128,4096]{1,0:T(8,128)(2,1)} collective-permute-done((bf16[128,4096]{1,0:T(8,128)(2,1)}, bf16[128,4096]{1,0:T(8,128)(2,1)}, u32[]{:S(2)}, u32[]{:S(2)}) %collective-permute-start) | collective-permute-done | bytes 1048608 | tf_op jit(solution)/shard_map/ppermute | solution.py:137
  38.4 1.7 fusion.55
  40.2 2.8 %fusion.53 = f32[128,512]{1,0:T(8,128)} fusion(bf16[128,4096]{1,0:T(8,128)(2,1)} %collective-permute-done, bf16[4096,512]{1,0:T(8,128)(2,1)S(1)} %copy-done.1), kind=kOutput, calls=%fused_computation.159 | convolution fusion | flops 536870912 | bytes 5505024 | tf_op jit(solution)/shard_map/dot_general | solution.py:36
  45.9 15.3 %fusion.13 = f32[256,4096]{1,0:T(8,128)S(1)} fusion(bf16[4096,4096]{1,0:T(8,128)(2,1)} %param.11, bf16[128,4096]{1,0:T(8,128)(2,1)} %collective-permute-done, bf16[128,4096]{1,0:T(8,128)(2,1)S(1)} %copy-done.6), kind=kOutput, calls=%fused_computation.21 | convolution fusion | flops 8594128896 | bytes 39845888 | tf_op jit(solution)/shard_map/dot_general | solution.py:36
  61.2 4.3 %broadcast_in_dim.276 = f32[4,128,4096]{2,1,0:T(8,128)} broadcast(f32[]{:T(128)} %constant.212.clone.1), dimensions={} | broadcast | bytes 8388612 | tf_op jit(solution)/shard_map/broadcast_in_dim | solution.py:133
  70.5 14.2 %fusion.3 = f32[4,128,4096]{2,1,0:T(8,128)} fusion(f32[4,128,4096]{2,1,0:T(8,128)} %fusion.11, s32[]{:T(128)S(6)} %select_n.276, bf16[128,4096]{1,0:T(8,128)(2,1)S(1)} %collective-permute-done.1, bf16[4096,4096]{1,0:T(8,128)(2,1)} %param.11), kind=kOutput, calls=%fused_computation.7 | convolution fusion | flops 4294967296 | bytes 36700164 | tf_op jit(solution)/shard_map/dot_general | solution.py:36
  86.8 2.9 %fusion.56 = f32[128,512]{1,0:T(8,128)S(1)} fusion(bf16[128,4096]{1,0:T(8,128)(2,1)S(1)} %collective-permute-done.1, bf16[4096,512]{1,0:T(8,128)(2,1)} %param.12), kind=kOutput, calls=%fused_computation.162 | convolution fusion | flops 536870912 | bytes 5505024 | tf_op jit(solution)/shard_map/dot_general | solution.py:36
  92.4 3.0 %collective-permute-done.2 = bf16[128,4096]{1,0:T(8,128)(2,1)S(1)} collective-permute-done((bf16[128,4096]{1,0:T(8,128)(2,1)S(1)}, bf16[128,4096]{1,0:T(8,128)(2,1)S(1)}, u32[]{:S(2)}, u32[]{:S(2)}) %collective-permute-start.2) | collective-permute-done | bytes 1048608 | tf_op jit(solution)/shard_map/ppermute | solution.py:137
  95.4 14.2 %fusion.2 = f32[4,128,4096]{2,1,0:T(8,128)} fusion(f32[4,128,4096]{2,1,0:T(8,128)} %fusion.3, s32[]{:T(128)S(6)} %select_n.281, bf16[128,4096]{1,0:T(8,128)(2,1)S(1)} %collective-permute-done.2, bf16[4096,4096]{1,0:T(8,128)(2,1)} %param.11), kind=kOutput, calls=%fused_computation.5 | convolution fusion | flops 4294967296 | bytes 36700164 | tf_op jit(solution)/shard_map/dot_general | solution.py:36
  111.7 2.9 %fusion.59 = f32[128,512]{1,0:T(8,128)S(1)} fusion(bf16[128,4096]{1,0:T(8,128)(2,1)S(1)} %collective-permute-done.2, bf16[4096,512]{1,0:T(8,128)(2,1)} %param.12), kind=kOutput, calls=%fused_computation.165 | convolution fusion | flops 536870912 | bytes 5505024 | tf_op jit(solution)/shard_map/dot_general | solution.py:36
  118.2 2.6 %all_gather.17 = bf16[512,512]{1,0:T(8,128)(2,1)S(1)} all-gather(bf16[256,512]{1,0:T(8,128)(2,1)S(1)} %copy-done.9), channel_id=1, replica_groups=mesh['groups'=2,'tensor'=4,'seq'=2,'load'=2] {'load'}, dimensions={0}, use_global_device_ids=true | all-gather | bytes 786432 | tf_op jit(solution)/shard_map/all_gather | solution.py:128
  123.6 8.4 %collective-permute-done.4 = f32[128,576]{1,0:T(8,128)S(1)} collective-permute-done((f32[128,576]{1,0:T(8,128)S(1)}, f32[128,576]{1,0:T(8,128)S(1)}, u32[]{:S(2)}, u32[]{:S(2)}) %collective-permute-start.4) | collective-permute-done | bytes 294944 | tf_op jit(solution)/shard_map/ppermute | solution.py:103
  132.4 13.1 %all-gather = bf16[128,256]{0,1:T(8,128)(2,1)S(1)} all-gather(bf16[128,64]{0,1:T(8,128)(2,1)S(1)} %copy.81), channel_id=2, replica_groups=mesh['groups'=2,'tensor'=4,'seq'=2,'load'=2] {'tensor'}, dimensions={1}, use_global_device_ids=true | all-gather | bytes 81920 | tf_op jit(solution)/shard_map/all_gather | solution.py:190
  146.5 15.5 %all_gather.18 = bf16[128,2048]{1,0:T(8,128)(2,1)S(1)} all-gather(bf16[128,512]{1,0:T(8,128)(2,1)S(1)} %fusion.25), channel_id=1, replica_groups=mesh['groups'=2,'tensor'=4,'seq'=2,'load'=2] {'tensor'}, dimensions={1}, use_global_device_ids=true | all-gather | bytes 655360 | tf_op jit(solution)/shard_map/all_gather | solution.py:202
  165.6 5.7 %collective-permute-done.5 = bf16[128,4,128]{2,0,1:T(8,128)(2,1)S(1)} collective-permute-done((bf16[128,4,128]{2,0,1:T(8,128)(2,1)}, bf16[128,4,128]{2,0,1:T(8,128)(2,1)S(1)}, u32[]{:S(2)}, u32[]{:S(2)}) %collective-permute-start.5) | collective-permute-done | bytes 131104 | tf_op jit(solution)/shard_map/ppermute | solution.py:23
  171.3 2.9 %fusion.62 = f32[128,4096]{1,0:T(8,128)S(1)} fusion(bf16[128,512]{0,1:T(8,128)(2,1)S(1)} %bitcast.152, bf16[512,4096]{1,0:T(8,128)(2,1)} %all-gather.3.cloned.1.call-done), kind=kOutput, calls=%fused_computation.168 | convolution fusion | flops 536870912 | bytes 6422528 | tf_op jit(solution)/shard_map/dot_general | solution.py:36
  174.3 4.3 %collective-permute-done.6 = bf16[128,4,128]{2,0,1:T(8,128)(2,1)} collective-permute-done((bf16[128,4,128]{2,0,1:T(8,128)(2,1)S(1)}, bf16[128,4,128]{2,0,1:T(8,128)(2,1)}, u32[]{:S(2)}, u32[]{:S(2)}) %collective-permute-start.6) | collective-permute-done | bytes 131104 | tf_op jit(solution)/shard_map/ppermute | solution.py:23
  187.6 1.8 add.327
  190.6 4.4 %fusion.22 = bf16[16,8,32,128]{3,1,2,0:T(8,128)(2,1)S(1)} fusion(f32[16,8,32,128]{3,2,1,0:T(8,128)S(1)} %bitcast.148, f32[128,4095]{1,0:T(8,128)S(1)} %get-tuple-element.58, f32[128,1]{1,0:T(8,128)S(1)} %get-tuple-element.60, f32[128,1]{1,0:T(8,128)S(1)} %get-tuple-element.59, f32[128,4095]{1,0:T(8,128)S(1)} %get-tuple-element.57, f32[128,4096]{1,0:T(8,128)S(1)} %add.327, ...), kind=kLoop, calls=%fused_computation.30 | loop fusion | flops 3670016 | bytes 11538432
  195.2 2.3 %fusion.20 = f32[2,512,128,16]{2,1,3,0:T(8,128)S(1)} fusion(bf16[128,2,16,128]{3,2,1,0:T(8,128)(2,1)S(1)} %bitcast.146, bf16[1024,4,128]{2,0,1:T(8,128)(2,1)} %constant_dynamic-update-slice_fusion, s32[]{:T(128)S(6)} %select_n.307), kind=kOutput, calls=%fused_computation.28 | convolution fusion | flops 536870912 | bytes 9699332 | tf_op jit(solution)/shard_map/qghd,kgd->ghqk/dot_general | solution.py:225
  197.5 4.6 %fusion.49 = (f32[2,16,128]{2,1,0:T(8,128)S(1)}, bf16[2,16,128,512]{2,3,1,0:T(8,128)(2,1)S(1)}) fusion(f32[2,512,128,16]{2,1,3,0:T(8,128)S(1)} %fusion.20, pred[128,512]{0,1:T(8,128)(4,1)S(1)} %copy-done.13), kind=kOutput, calls=%fused_computation.155 | output fusion | flops 16777728 | bytes 12664832 | tf_op jit(solution)/shard_map/sub | solution.py:230
  (143 shorter events, 46.0 us)
Async XLA Ops:
  8.0 4.9 %copy-start = (bf16[4096,128]{1,0:T(8,128)(2,1)S(1)}, bf16[4096,128]{1,0:T(8,128)(2,1)}, u32[]{:S(2)}) copy-start(bf16[4096,128]{1,0:T(8,128)(2,1)} %param.13) | copy-start | bytes 3145732
  8.0 6.6 %copy-start.5 = (bf16[128,4096]{1,0:T(8,128)(2,1)S(1)}, bf16[128,4096]{1,0:T(8,128)(2,1)}, u32[]{:S(2)}) copy-start(bf16[128,4096]{1,0:T(8,128)(2,1)} %param.10) | copy-start | bytes 3145732
  8.0 6.6 %copy-start.2 = (bf16[4096,128]{1,0:T(8,128)(2,1)S(1)}, bf16[4096,128]{1,0:T(8,128)(2,1)}, u32[]{:S(2)}) copy-start(bf16[4096,128]{1,0:T(8,128)(2,1)} %param.14) | copy-start | bytes 3145732
  8.0 7.2 %copy-start.16 = (s32[4]{0:T(128)S(1)}, s32[4]{0:T(128)}, u32[]{:S(2)}) copy-start(s32[4]{0:T(128)} %param.17) | copy-start | bytes 52
  8.0 7.2 %copy-start.17 = (s32[4]{0:T(128)S(1)}, s32[4]{0:T(128)}, u32[]{:S(2)}) copy-start(s32[4]{0:T(128)} %param.19) | copy-start | bytes 52
  8.1 163.3 %all-gather.3.cloned.1.call-start = ((), (), s32[]{:S(2)}) async-start(), calls=%async_computation.2 | async-start | bytes 6291456 | tf_op jit(solution)/shard_map/all_gather | solution.py:127
  8.1 28.6 %collective-permute-start = (bf16[128,4096]{1,0:T(8,128)(2,1)}, bf16[128,4096]{1,0:T(8,128)(2,1)}, u32[]{:S(2)}, u32[]{:S(2)}) collective-permute-start(bf16[128,4096]{1,0:T(8,128)(2,1)} %param.10), channel_id=1, source_target_pairs={{0,4},{4,8},{8,12},{12,0},{1,5},{5,9},{9,13},{13,1},{2,6},{6,10},{... | collective-permute-start | bytes 3145736 | tf_op jit(solution)/shard_map/ppermute | solution.py:137
  11.2 176.4 %reduce-scatter.2.cloned.1.call-start = ((), (), s32[]{:S(2)}) async-start(), calls=%async_computation.1 | async-start | bytes 10485760 | tf_op jit(solution)/shard_map/reduce_scatter | solution.py:177
  19.3 20.9 %copy-start.1 = (bf16[4096,512]{1,0:T(8,128)(2,1)S(1)}, bf16[4096,512]{1,0:T(8,128)(2,1)}, u32[]{:S(2)}) copy-start(bf16[4096,512]{1,0:T(8,128)(2,1)} %param.12) | copy-start | bytes 12582916
  40.2 5.7 %copy-start.6 = (bf16[128,4096]{1,0:T(8,128)(2,1)S(1)}, bf16[128,4096]{1,0:T(8,128)(2,1)}, u32[]{:S(2)}) copy-start(bf16[128,4096]{1,0:T(8,128)(2,1)} %param.10) | copy-start | bytes 3145732
  43.0 26.4 %collective-permute-start.1 = (bf16[128,4096]{1,0:T(8,128)(2,1)}, bf16[128,4096]{1,0:T(8,128)(2,1)S(1)}, u32[]{:S(2)}, u32[]{:S(2)}) collective-permute-start(bf16[128,4096]{1,0:T(8,128)(2,1)} %collective-permute-done), channel_id=1, source_target_pairs={{0,4},{4,8},{8,12},{12,0},{1,5},{5,9},{9,13},{13,1},{2,6},{6,10},{... | collective-permute-start | bytes 3145736 | tf_op jit(solution)/shard_map/ppermute | solution.py:137
  65.5 1.5 copy-start.7
  69.3 16.0 %copy-start.3 = (bf16[4096,128]{1,0:T(8,128)(2,1)S(1)}, bf16[4096,128]{1,0:T(8,128)(2,1)}, u32[]{:S(2)}) copy-start(bf16[4096,128]{1,0:T(8,128)(2,1)} %param.14) | copy-start | bytes 3145732
  69.4 26.1 %collective-permute-start.2 = (bf16[128,4096]{1,0:T(8,128)(2,1)S(1)}, bf16[128,4096]{1,0:T(8,128)(2,1)S(1)}, u32[]{:S(2)}, u32[]{:S(2)}) collective-permute-start(bf16[128,4096]{1,0:T(8,128)(2,1)S(1)} %collective-permute-done.1), channel_id=1, source_target_pairs={{0,4},{4,8},{8,12},{12,0},{1,5},{5,9},{9,13},{13,1},{2,6},{6,10},{... | collective-permute-start | bytes 3145736 | tf_op jit(solution)/shard_map/ppermute | solution.py:137
  86.8 2.9 %copy-start.12 = (f32[128,32]{1,0:T(8,128)S(1)}, f32[128,32]{1,0:T(8,128)}, u32[]{:S(2)}) copy-start(f32[128,32]{1,0:T(8,128)} %copy.74) | copy-start | bytes 49156
  109.7 1.2 copy-start.4
  111.7 6.5 %copy-start.9 = (bf16[256,512]{1,0:T(8,128)(2,1)S(1)}, bf16[256,512]{1,0:T(8,128)(2,1)}, u32[]{:S(2)}) copy-start(bf16[256,512]{1,0:T(8,128)(2,1)} %param.16) | copy-start | bytes 786436
  116.8 3.9 %collective-permute-start.3 = (f32[2,128,576]{1,2,0:T(8,128)S(1)}, f32[2,128,576]{1,2,0:T(8,128)S(1)}, u32[]{:S(2)}, u32[]{:S(2)}) collective-permute-start(f32[2,128,576]{1,2,0:T(8,128)S(1)} %dynamic-slice_bitcast_fusion), channel_id=1, source_target_pairs={{0,1},{1,0},{2,3},{3,2},{4,5},{5,4},{6,7},{7,6},{8,9},{9,8},{10,11... | collective-permute-start | bytes 1769480 | tf_op jit(solution)/shard_map/ppermute | solution.py:103
  122.2 9.8 %collective-permute-start.4 = (f32[128,576]{1,0:T(8,128)S(1)}, f32[128,576]{1,0:T(8,128)S(1)}, u32[]{:S(2)}, u32[]{:S(2)}) collective-permute-start(f32[128,576]{1,0:T(8,128)S(1)} %bitcast.154), channel_id=1, source_target_pairs={{0,2},{2,0},{1,3},{3,1},{4,6},{6,4},{5,7},{7,5},{8,10},{10,8},{9,1... | collective-permute-start | bytes 884744 | tf_op jit(solution)/shard_map/ppermute | solution.py:103
  146.5 15.6 %copy-start.8 = (bf16[128,512]{1,0:T(8,128)(2,1)}, bf16[128,512]{1,0:T(8,128)(2,1)S(1)}, u32[]{:S(2)}) copy-start(bf16[128,512]{1,0:T(8,128)(2,1)S(1)} %fusion.25) | copy-start | bytes 393220
  163.2 8.1 %collective-permute-start.5 = (bf16[128,4,128]{2,0,1:T(8,128)(2,1)}, bf16[128,4,128]{2,0,1:T(8,128)(2,1)S(1)}, u32[]{:S(2)}, u32[]{:S(2)}) collective-permute-start(bf16[128,4,128]{2,0,1:T(8,128)(2,1)} %pad_maximum_fusion), channel_id=1, source_target_pairs={{0,1},{1,2},{2,3},{3,0},{4,5},{5,6},{6,7},{7,4},{8,9},{9,10},{10,1... | collective-permute-start | bytes 393224 | tf_op jit(solution)/shard_map/ppermute | solution.py:23
  163.9 17.6 %collective-permute-start.7 = (bf16[128,4,128]{2,0,1:T(8,128)(2,1)}, bf16[128,4,128]{2,0,1:T(8,128)(2,1)}, u32[]{:S(2)}, u32[]{:S(2)}) collective-permute-start(bf16[128,4,128]{2,0,1:T(8,128)(2,1)} %pad_maximum_fusion), channel_id=1, source_target_pairs={{0,3},{1,0},{2,1},{3,2},{4,7},{5,4},{6,5},{7,6},{8,11},{9,8},{10,9... | collective-permute-start | bytes 393224 | tf_op jit(solution)/shard_map/ppermute | solution.py:25
  171.3 7.3 %collective-permute-start.6 = (bf16[128,4,128]{2,0,1:T(8,128)(2,1)S(1)}, bf16[128,4,128]{2,0,1:T(8,128)(2,1)}, u32[]{:S(2)}, u32[]{:S(2)}) collective-permute-start(bf16[128,4,128]{2,0,1:T(8,128)(2,1)S(1)} %collective-permute-done.5), channel_id=1, source_target_pairs={{0,1},{1,2},{2,3},{3,0},{4,5},{5,6},{6,7},{7,4},{8,9},{9,10},{10,1... | collective-permute-start | bytes 393224 | tf_op jit(solution)/shard_map/ppermute | solution.py:23
  195.2 2.3 %copy-start.13 = (pred[128,512]{0,1:T(8,128)(4,1)S(1)}, pred[128,512]{0,1:T(8,128)(4,1)}, u32[]{:S(2)}) copy-start(pred[128,512]{0,1:T(8,128)(4,1)} %fusion.26) | copy-start | bytes 196612
  (4 other events, 3.1 us)
Sparse Core Ops, SparseCore 0:
  11.3 15.5 all-gather.2
Sparse Core Ops, SparseCore 1:
  109.8 75.2 reduce-scatter.1
